TPU v7x, 256 devices: a whole 4x4x8 slice. The times are simulated.
256 devices in a mesh: section: 8 (over x, core), dp: 32 (over y, z).
Axes of the slice: x: 4, y: 4, z: 8, core: 2. Of those that a mesh axis runs over, the one named last changes fastest.
Arguments:
- resid_in: bfloat16 [4, 1024, 2048], P(None, 'dp'), may hold values from -10 to 10
- dest_row: int32 [4, 1024], replicated, may hold values from 0 to 1023, as said below
- doc_ids: int32 [4, 1024], P(None, 'dp'), may hold values from 0 to 1023, as said below
- cotangent: bfloat16 [4, 1024, 2048], P(None, 'dp'), may hold values from -0.119628906 to 0.119628906
- gain: float32 [8, 2048], P('section'), may hold values from 0.5 to 1.5
- steer: float32 [8, 2048], P('section'), may hold values from -3 to 3
- w_query: bfloat16 [8, 2048, 1024], P('section', 'dp'), may hold values from -1 to 1
- w_keyval: bfloat16 [8, 2048, 512], P('section', 'dp'), may hold values from -1 to 1
- w_out: bfloat16 [8, 1024, 2048], P('section', None, 'dp'), may hold values from -0.1875 to 0.1875
Outputs:
- hidden_out: bfloat16 [8, 4, 1024, 2048], P('section', None, 'dp')
- grad_steer: float32 [8, 2048], P('section')
Inputs may be any that keep to these rules, and one draw needn't show every extreme that they name: Each row of dest_row is a permutation of 0 to 1023. Counting the tokens of one aligned block of 32 input tokens that go to one aligned block of 32 packed rows, no count exceeds 2, and some reach it in every micro-batch. doc_ids never falls along a row; every value is a row index r at which doc_ids equals r; each aligned block of 32 rows begins a document, so no document crosses such a block.
All inputs are finite; a program needn't handle non-finite values.
Results may differ from a plain program's by a relative error of at most 0.02.
Values may be sent and summed in bfloat16 or wider, within the bound.
No kernel may reach another device: no remote copies, remote signals or barrier semaphores. Data moves between devices by JAX's collectives and lax.ppermute only.
A program may use at most 64 MiB of HBM per device.

v0:
```python
import jax
import jax.numpy as jnp
from jax import lax
from jax.sharding import PartitionSpec as P

HD = 64
ROPE_BASE = 500000.0
EPSILON = 1e-05
MASKED = -1e30


def shifted(block, axis, distance):
    devices = range(lax.axis_size(axis))
    route = [(i - distance, i) for i in devices if i - distance in devices]
    return lax.ppermute(block, axis, route)


def rotate(values, positions):
    half_size = values.shape[-1] // 2
    freq_index = jnp.arange(half_size, dtype=jnp.float32)
    inverse = ROPE_BASE ** (-2.0 * freq_index / values.shape[-1])
    angles = positions.astype(jnp.float32)[:, None] * inverse[None, :]
    cosine = jnp.cos(angles)[:, None, :]
    sine_part = jnp.sin(angles)[:, None, :]
    first_half = values[..., :half_size]
    second = values[..., half_size:]
    return jnp.concatenate(
        [first_half * cosine - second * sine_part, second * cosine + first_half * sine_part],
        axis=-1,
    )


def layer(hidden_in, steering, gain_row, w_query, w_keyval, w_out, positions, documents):
    row_count = hidden_in.shape[0]
    head_size = HD
    kv_heads = w_keyval.shape[1] // (2 * head_size)
    query_heads = w_query.shape[1] // head_size
    group_size = query_heads // kv_heads
    residual = hidden_in.astype(jnp.float32) + steering
    normed = (
        residual
        * lax.rsqrt(jnp.mean(residual * residual, axis=-1, keepdims=True) + EPSILON)
        * gain_row
    ).astype(jnp.bfloat16)
    queries = jnp.dot(normed, w_query, preferred_element_type=jnp.float32).reshape(
        row_count, query_heads, head_size
    )
    keyval = jnp.dot(normed, w_keyval, preferred_element_type=jnp.float32)
    key_rows = rotate(
        keyval[:, : kv_heads * head_size].reshape(row_count, kv_heads, head_size), positions
    ).astype(jnp.bfloat16)
    values = (
        keyval[:, kv_heads * head_size :]
        .reshape(row_count, kv_heads, head_size)
        .astype(jnp.bfloat16)
    )
    queries = (
        rotate(queries, positions)
        .astype(jnp.bfloat16)
        .reshape(row_count, kv_heads, group_size, head_size)
    )
    scores = jnp.einsum(
        "rkgd,skd->kgrs", queries, key_rows, preferred_element_type=jnp.float32
    ) * head_size ** (-0.5)
    row_index = jnp.arange(row_count)
    allowed = (documents[:, None] == documents[None, :]) & (
        row_index[:, None] >= row_index[None, :]
    )
    scores = jnp.where(allowed[None, None], scores, MASKED)
    peak = jnp.max(scores, axis=-1, keepdims=True)
    weights = jnp.exp(scores - peak)
    weights = (weights / jnp.sum(weights, axis=-1, keepdims=True)).astype(jnp.bfloat16)
    mixed_heads = jnp.einsum(
        "kgrs,skd->rkgd", weights, values, preferred_element_type=jnp.float32
    ).astype(jnp.bfloat16)
    mixed_heads = mixed_heads.reshape(row_count, query_heads * head_size)
    return (residual + jnp.dot(mixed_heads, w_out, preferred_element_type=jnp.float32)).astype(
        jnp.bfloat16
    )


def plan_slots(target, device, row_count, capacity, dp_count):
    target_grid = target.reshape(dp_count, row_count)
    target_dev = target_grid // row_count
    target_off = target_grid % row_count
    row_order = jnp.arange(row_count, dtype=jnp.int32)
    matching = target_dev[:, :, None] == target_dev[:, None, :]
    earlier = row_order[None, :] < row_order[:, None]
    rank_ids = jnp.sum((matching & earlier[None]).astype(jnp.int32), axis=2)
    slot_ids = target_dev * capacity + rank_ids
    own_slot = lax.dynamic_index_in_dim(slot_ids, device, 0, keepdims=False)
    column_ids = jnp.arange(dp_count, dtype=jnp.int32)[:, None] * capacity + rank_ids
    landing = (target_dev == device)[None] & (target_off[None] == row_order[:, None, None])
    source_col = jnp.sum(jnp.where(landing, column_ids[None], 0), axis=(1, 2))
    return (own_slot, source_col)


def pack_rows(source_rows, own_slot, slot_count):
    selector = (jnp.arange(slot_count, dtype=jnp.int32)[:, None] == own_slot[None, :]).astype(
        jnp.bfloat16
    )
    return jnp.dot(selector, source_rows, preferred_element_type=jnp.float32).astype(jnp.bfloat16)


def unpack_rows(arrived, source_col):
    selector = (
        source_col[:, None] == jnp.arange(arrived.shape[0], dtype=jnp.int32)[None, :]
    ).astype(jnp.bfloat16)
    return jnp.dot(selector, arrived, preferred_element_type=jnp.float32).astype(jnp.bfloat16)


def body(resid_in, dest_row, doc_ids, cotangent, gain, steer, w_query, w_keyval, w_out):
    dp_count = lax.axis_size("dp")
    section_count = lax.axis_size("section")
    device = lax.axis_index("dp")
    section_idx = lax.axis_index("section")
    micro_count, row_count, width = resid_in.shape
    capacity = row_count // dp_count + 1
    slot_count = dp_count * capacity
    full_query, full_keyval, full_out = (
        lax.all_gather(w_query[0], "dp", axis=0, tiled=True),
        lax.all_gather(w_keyval[0], "dp", axis=0, tiled=True),
        lax.all_gather(w_out[0], "dp", axis=1, tiled=True),
    )
    gain_row = gain[0]
    steering = steer[0]
    plans = [
        plan_slots(dest_row[micro_idx], device, row_count, capacity, dp_count)
        for micro_idx in range(micro_count)
    ]
    pieces = []
    for micro_idx in range(micro_count):
        packed = pack_rows(resid_in[micro_idx], plans[micro_idx][0], slot_count).reshape(
            dp_count, capacity, width
        )
        arrived = lax.all_to_all(packed, "dp", split_axis=0, concat_axis=0, tiled=True)
        pieces.append(unpack_rows(arrived.reshape(slot_count, width), plans[micro_idx][1]))
    grouped = jnp.stack(pieces)
    global_rows = device * row_count + jnp.arange(row_count, dtype=jnp.int32)
    position_table = global_rows[None, :] - doc_ids

    def run_layer(hidden_in, steer_vec, positions, documents):
        return layer(
            hidden_in, steer_vec, gain_row, full_query, full_keyval, full_out, positions, documents
        )

    zero_block = jnp.zeros((row_count, width), jnp.bfloat16)
    step_count = micro_count + section_count - 1

    def forward_step(carry, step_idx):
        incoming, kept, produced = carry
        micro_idx = step_idx - section_idx
        active = (micro_idx >= 0) & (micro_idx < micro_count)
        chosen = jnp.clip(micro_idx, 0, micro_count - 1)
        first_in = lax.dynamic_index_in_dim(grouped, chosen, 0, keepdims=False)
        hidden_in = jnp.where(section_idx == 0, first_in, incoming)
        positions = lax.dynamic_index_in_dim(position_table, chosen, 0, keepdims=False)
        documents = lax.dynamic_index_in_dim(doc_ids, chosen, 0, keepdims=False)
        hidden_new = lax.cond(
            active, lambda: run_layer(hidden_in, steering, positions, documents), lambda: zero_block
        )
        old_kept = lax.dynamic_index_in_dim(kept, chosen, 0, keepdims=False)
        kept = lax.dynamic_update_index_in_dim(
            kept, jnp.where(active, hidden_in, old_kept), chosen, 0
        )
        old_out = lax.dynamic_index_in_dim(produced, chosen, 0, keepdims=False)
        produced = lax.dynamic_update_index_in_dim(
            produced, jnp.where(active, hidden_new, old_out), chosen, 0
        )
        sent = shifted(hidden_new, "section", 1)
        return ((sent, kept, produced), None)

    empty_stack = jnp.zeros((micro_count, row_count, width), jnp.bfloat16)
    (unused_in, kept, produced), unused_ys = lax.scan(
        forward_step,
        (zero_block, empty_stack, empty_stack),
        jnp.arange(step_count, dtype=jnp.int32),
    )

    def backward_step(carry, step_idx):
        incoming, grad_sum = carry
        micro_idx = step_idx - (section_count - 1 - section_idx)
        active = (micro_idx >= 0) & (micro_idx < micro_count)
        chosen = jnp.clip(micro_idx, 0, micro_count - 1)
        last_in = lax.dynamic_index_in_dim(cotangent, chosen, 0, keepdims=False)
        upstream = jnp.where(section_idx == section_count - 1, last_in, incoming)
        positions = lax.dynamic_index_in_dim(position_table, chosen, 0, keepdims=False)
        documents = lax.dynamic_index_in_dim(doc_ids, chosen, 0, keepdims=False)
        saved_in = lax.dynamic_index_in_dim(kept, chosen, 0, keepdims=False)

        def differentiate():

            def local(hidden_in, steer_vec):
                return run_layer(hidden_in, steer_vec, positions, documents)

            unused_out, pullback = jax.vjp(local, saved_in, steering)
            return pullback(upstream)

        grad_in, steer_part = lax.cond(
            active, differentiate, lambda: (zero_block, jnp.zeros_like(steering))
        )
        sent = shifted(grad_in, "section", -1)
        return ((sent, grad_sum + steer_part), None)

    (unused_grad, grad_sum), unused_zs = lax.scan(
        backward_step,
        (zero_block, jnp.zeros_like(steering)),
        jnp.arange(step_count, dtype=jnp.int32),
    )
    total = lax.psum(grad_sum, "dp")
    return (produced[None], total[None])


def solution(mesh):
    in_specs = (
        P(None, "dp", None),
        P(),
        P(None, "dp"),
        P(None, "dp", None),
        P("section", None),
        P("section", None),
        P("section", "dp", None),
        P("section", "dp", None),
        P("section", None, "dp"),
    )
    out_specs = (P("section", None, "dp", None), P("section", None))
    return jax.shard_map(body, mesh=mesh, in_specs=in_specs, out_specs=out_specs, check_vma=False)
```

profile of v0, /device:TPU:0, one launch (start us, length us, event | category | flops | bytes accessed | tf_op | source)
XLA Modules:
  0.0 934.9 jit_solution(14943596170563933842)
XLA Ops:
  15.6 9.8 %all-to-all-start = ((bf16[32,2,2048]{2,1,0:T(2,128)(2,1)}), bf16[32,2,2048]{2,1,0:T(2,128)(2,1)S(1)}, u32[]{:S(2)}, u32[]{:S(2)}) async-start(bf16[32,2,2048]{2,1,0:T(2,128)(2,1)} %reshape.889), calls=%async_computation | async-start | bytes 524288 | tf_op jit(solution)/shard_map/all_to_all | solution.py:136
  29.3 9.8 %all-to-all-done = bf16[32,2,2048]{2,1,0:T(2,128)(2,1)S(1)} async-done(((bf16[32,2,2048]{2,1,0:T(2,128)(2,1)}), bf16[32,2,2048]{2,1,0:T(2,128)(2,1)S(1)}, u32[]{:S(2)}, u32[]{:S(2)}) %all-to-all-start) | async-done | bytes 262176 | tf_op jit(solution)/shard_map/all_to_all | solution.py:136
  46.1 10.0 %all-to-all-done.1 = bf16[32,2,2048]{2,1,0:T(2,128)(2,1)S(1)} async-done(((bf16[32,2,2048]{2,1,0:T(2,128)(2,1)}), bf16[32,2,2048]{2,1,0:T(2,128)(2,1)S(1)}, u32[]{:S(2)}, u32[]{:S(2)}) %all-to-all-start.1) | async-done | bytes 262176 | tf_op jit(solution)/shard_map/all_to_all | solution.py:136
  62.5 12.0 %all-to-all-done.2 = bf16[32,2,2048]{2,1,0:T(2,128)(2,1)S(1)} async-done(((bf16[32,2,2048]{2,1,0:T(2,128)(2,1)}), bf16[32,2,2048]{2,1,0:T(2,128)(2,1)S(1)}, u32[]{:S(2)}, u32[]{:S(2)}) %all-to-all-start.2) | async-done | bytes 262176 | tf_op jit(solution)/shard_map/all_to_all | solution.py:136
  82.6 10.3 %all-to-all-done.3 = bf16[32,2,2048]{2,1,0:T(2,128)(2,1)S(1)} async-done(((bf16[32,2,2048]{2,1,0:T(2,128)(2,1)}), bf16[32,2,2048]{2,1,0:T(2,128)(2,1)S(1)}, u32[]{:S(2)}, u32[]{:S(2)}) %all-to-all-start.3) | async-done | bytes 262176 | tf_op jit(solution)/shard_map/all_to_all | solution.py:136
  106.4 75.2 %all-gather.9.cloned.1.call-done = bf16[1,2048,1024]{2,1,0:T(8,128)(2,1)} async-done(((bf16[1,64,1024]{2,1,0:T(8,128)(2,1)}), bf16[1,2048,1024]{2,1,0:T(8,128)(2,1)}) %all-gather.9.cloned.1.call-update) | async-done | bytes 4194320 | tf_op jit(solution)/shard_map/all_gather | solution.py:121
  188.2 71.0 %all-gather.7.cloned.1.call-done = bf16[1,2048,512]{2,1,0:T(8,128)(2,1)} async-done(((bf16[1,64,512]{2,1,0:T(8,128)(2,1)}), bf16[1,2048,512]{2,1,0:T(8,128)(2,1)}) %all-gather.7.cloned.1.call-update) | async-done | bytes 2097168 | tf_op jit(solution)/shard_map/all_gather | solution.py:122
  259.3 156.2 %while.30 = (s32[]{:T(128)}, bf16[32,2048]{1,0:T(8,128)(2,1)S(1)}, bf16[4,32,2048]{2,1,0:T(8,128)(2,1)S(1)}, bf16[4,32,2048]{2,1,0:T(8,128)(2,1)S(1)}, s32[11]{0...) while((s32[]{:T(128)}, bf16[32,2048]{1,0:T(8,128)(2,1)S(1)}, ...), condition=%wide.region_14.15_spmd, body=%wide.region_8.14_spmd.sunk | while | flops 343888544 | bytes 14992390 | solution.py:174
  260.6 11.3 %conditional.5 = (bf16[32,2048]{1,0:T(8,128)(2,1)S(1)}) conditional(s32[]{:T(128)} %convert_element_type.419, () %tuple.130, (bf16[32,2048]{1,0:T(8,128)(2,1)S(1)}, f32[1,2048]{1,0:T(1,128)S(1)}, f32[1,2048]{1,0:T(1,128)S(1)}, bf16[2048,512]{1,0:T(8,128)(2,1)}, s32[4,32]{1,0:T(4,128)}, /*index=5*/s32[]{:T(128)}, s32[4,32]{1,0:T(4,128)}, ...), branch_computations={%region_9.9_spmd, %region_10.13_spmd} | conditional | flops 343691936 | bytes 12894860 | solution.py:159
  275.6 11.3 %conditional.5 = (bf16[32,2048]{1,0:T(8,128)(2,1)S(1)}) conditional(s32[]{:T(128)} %convert_element_type.419, () %tuple.130, (bf16[32,2048]{1,0:T(8,128)(2,1)S(1)}, f32[1,2048]{1,0:T(1,128)S(1)}, f32[1,2048]{1,0:T(1,128)S(1)}, bf16[2048,512]{1,0:T(8,128)(2,1)}, s32[4,32]{1,0:T(4,128)}, /*index=5*/s32[]{:T(128)}, s32[4,32]{1,0:T(4,128)}, ...), branch_computations={%region_9.9_spmd, %region_10.13_spmd} | conditional | flops 343691936 | bytes 12894860 | solution.py:159
  291.5 11.3 %conditional.5 = (bf16[32,2048]{1,0:T(8,128)(2,1)S(1)}) conditional(s32[]{:T(128)} %convert_element_type.419, () %tuple.130, (bf16[32,2048]{1,0:T(8,128)(2,1)S(1)}, f32[1,2048]{1,0:T(1,128)S(1)}, f32[1,2048]{1,0:T(1,128)S(1)}, bf16[2048,512]{1,0:T(8,128)(2,1)}, s32[4,32]{1,0:T(4,128)}, /*index=5*/s32[]{:T(128)}, s32[4,32]{1,0:T(4,128)}, ...), branch_computations={%region_9.9_spmd, %region_10.13_spmd} | conditional | flops 343691936 | bytes 12894860 | solution.py:159
  308.0 11.3 %conditional.5 = (bf16[32,2048]{1,0:T(8,128)(2,1)S(1)}) conditional(s32[]{:T(128)} %convert_element_type.419, () %tuple.130, (bf16[32,2048]{1,0:T(8,128)(2,1)S(1)}, f32[1,2048]{1,0:T(1,128)S(1)}, f32[1,2048]{1,0:T(1,128)S(1)}, bf16[2048,512]{1,0:T(8,128)(2,1)}, s32[4,32]{1,0:T(4,128)}, /*index=5*/s32[]{:T(128)}, s32[4,32]{1,0:T(4,128)}, ...), branch_computations={%region_9.9_spmd, %region_10.13_spmd} | conditional | flops 343691936 | bytes 12894860 | solution.py:159
  327.0 16.6 %collective-permute-start = (bf16[32,2048]{1,0:T(8,128)(2,1)S(1)}, bf16[32,2048]{1,0:T(8,128)(2,1)S(1)}, u32[]{:S(2)}, u32[]{:S(2)}) collective-permute-start(bf16[32,2048]{1,0:T(8,128)(2,1)S(1)} %get-tuple-element.1094), channel_id=1, source_target_pairs={{0,32},{32,64},{64,96},{96,128},{128,160},{160,192},{192,224},{1,3... | collective-permute-start | bytes 393224 | tf_op jit(solution)/shard_map/while/body/eval_jaxpr/ppermute | solution.py:15
  353.6 16.6 %collective-permute-start = (bf16[32,2048]{1,0:T(8,128)(2,1)S(1)}, bf16[32,2048]{1,0:T(8,128)(2,1)S(1)}, u32[]{:S(2)}, u32[]{:S(2)}) collective-permute-start(bf16[32,2048]{1,0:T(8,128)(2,1)S(1)} %get-tuple-element.1094), channel_id=1, source_target_pairs={{0,32},{32,64},{64,96},{96,128},{128,160},{160,192},{192,224},{1,3... | collective-permute-start | bytes 393224 | tf_op jit(solution)/shard_map/while/body/eval_jaxpr/ppermute | solution.py:15
  380.2 10.2 %collective-permute-start = (bf16[32,2048]{1,0:T(8,128)(2,1)S(1)}, bf16[32,2048]{1,0:T(8,128)(2,1)S(1)}, u32[]{:S(2)}, u32[]{:S(2)}) collective-permute-start(bf16[32,2048]{1,0:T(8,128)(2,1)S(1)} %get-tuple-element.1094), channel_id=1, source_target_pairs={{0,32},{32,64},{64,96},{96,128},{128,160},{160,192},{192,224},{1,3... | collective-permute-start | bytes 393224 | tf_op jit(solution)/shard_map/while/body/eval_jaxpr/ppermute | solution.py:15
  400.4 14.2 %collective-permute-start = (bf16[32,2048]{1,0:T(8,128)(2,1)S(1)}, bf16[32,2048]{1,0:T(8,128)(2,1)S(1)}, u32[]{:S(2)}, u32[]{:S(2)}) collective-permute-start(bf16[32,2048]{1,0:T(8,128)(2,1)S(1)} %get-tuple-element.1094), channel_id=1, source_target_pairs={{0,32},{32,64},{64,96},{96,128},{128,160},{160,192},{192,224},{1,3... | collective-permute-start | bytes 393224 | tf_op jit(solution)/shard_map/while/body/eval_jaxpr/ppermute | solution.py:15
  416.3 438.7 %while.31 = (s32[]{:T(128)}, bf16[32,2048]{1,0:T(8,128)(2,1)S(1)}, f32[2048]{0:T(1024)}, s32[11]{0:T(128)}, s32[]{:T(128)}, /*index=5*/pred[]{:T(512)}, bf16[4,3...) while((s32[]{:T(128)}, bf16[32,2048]{1,0:T(8,128)(2,1)S(1)}, ...), condition=%wide.region_26.27_spmd.clone, body=%wide.region_15.26_spmd.clone.sunk | while | flops 551212288 | bytes 31677904 | solution.py:205
  453.8 13.3 %collective-permute-done.1 = bf16[32,2048]{1,0:T(8,128)(2,1)S(1)} collective-permute-done((bf16[32,2048]{1,0:T(8,128)(2,1)}, bf16[32,2048]{1,0:T(8,128)(2,1)S(1)}, u32[]{:S(2)}, u32[]{:S(2)}) %collective-permute-start.1) | collective-permute-done | bytes 131104 | tf_op jit(solution)/shard_map/while/body/eval_jaxpr/ppermute | solution.py:15
  495.5 207.9 %collective-permute-done.1 = bf16[32,2048]{1,0:T(8,128)(2,1)S(1)} collective-permute-done((bf16[32,2048]{1,0:T(8,128)(2,1)}, bf16[32,2048]{1,0:T(8,128)(2,1)S(1)}, u32[]{:S(2)}, u32[]{:S(2)}) %collective-permute-start.1) | collective-permute-done | bytes 131104 | tf_op jit(solution)/shard_map/while/body/eval_jaxpr/ppermute | solution.py:15
  705.2 30.4 %conditional.6 = (bf16[32,2048]{1,0:T(8,128)(2,1)}, f32[2048]{0:T(1024)S(1)}) conditional(s32[]{:T(128)} %convert_element_type.420, () %tuple.133, (pred[]{:T(512)}, s32[]{:T(128)}, bf16[4,32,2048]{2,1,0:T(8,128)(2,1)}, bf16[32,2048]{1,0:T(8,128)(2,1)S(1)}, bf16[1024,2048]{1,0:T(8,128)(2,1)}, /*index=5*/s32[4,32]{1,0:T(4,128)}, ...), branch_computations={%region_16.16_spmd, %region_17.25_spmd} | conditional | flops 551208192 | bytes 31128680 | solution.py:199
  743.9 30.4 %conditional.6 = (bf16[32,2048]{1,0:T(8,128)(2,1)}, f32[2048]{0:T(1024)S(1)}) conditional(s32[]{:T(128)} %convert_element_type.420, () %tuple.133, (pred[]{:T(512)}, s32[]{:T(128)}, bf16[4,32,2048]{2,1,0:T(8,128)(2,1)}, bf16[32,2048]{1,0:T(8,128)(2,1)S(1)}, bf16[1024,2048]{1,0:T(8,128)(2,1)}, /*index=5*/s32[4,32]{1,0:T(4,128)}, ...), branch_computations={%region_16.16_spmd, %region_17.25_spmd} | conditional | flops 551208192 | bytes 31128680 | solution.py:199
  782.5 30.4 %conditional.6 = (bf16[32,2048]{1,0:T(8,128)(2,1)}, f32[2048]{0:T(1024)S(1)}) conditional(s32[]{:T(128)} %convert_element_type.420, () %tuple.133, (pred[]{:T(512)}, s32[]{:T(128)}, bf16[4,32,2048]{2,1,0:T(8,128)(2,1)}, bf16[32,2048]{1,0:T(8,128)(2,1)S(1)}, bf16[1024,2048]{1,0:T(8,128)(2,1)}, /*index=5*/s32[4,32]{1,0:T(4,128)}, ...), branch_computations={%region_16.16_spmd, %region_17.25_spmd} | conditional | flops 551208192 | bytes 31128680 | solution.py:199
  821.2 30.4 %conditional.6 = (bf16[32,2048]{1,0:T(8,128)(2,1)}, f32[2048]{0:T(1024)S(1)}) conditional(s32[]{:T(128)} %convert_element_type.420, () %tuple.133, (pred[]{:T(512)}, s32[]{:T(128)}, bf16[4,32,2048]{2,1,0:T(8,128)(2,1)}, bf16[32,2048]{1,0:T(8,128)(2,1)S(1)}, bf16[1024,2048]{1,0:T(8,128)(2,1)}, /*index=5*/s32[4,32]{1,0:T(4,128)}, ...), branch_computations={%region_16.16_spmd, %region_17.25_spmd} | conditional | flops 551208192 | bytes 31128680 | solution.py:199
  855.0 73.4 %psum.7 = f32[1,2048]{1,0:T(1,128)} all-reduce(f32[1,2048]{1,0:T(1,128)} %bitcast.272), channel_id=1, replica_groups=mesh['section'=8,'dp'=32] {'dp'}, use_global_device_ids=true, to_apply=%region_27.28 | all-reduce | flops 2048 | bytes 16384 | tf_op jit(solution)/shard_map/psum | solution.py:210
  (597 shorter events, 359.1 us)
Async XLA Ops:
  7.2 92.8 %all-gather.11.cloned.1.call-start = ((), (), s32[]{:S(2)}) async-start(), calls=%async_computation.6 | async-start | bytes 4325376 | tf_op jit(solution)/shard_map/all_gather | solution.py:123
  7.9 173.7 %all-gather.9.cloned.1.call-start = ((), (), s32[]{:S(2)}) async-start(), calls=%async_computation.5 | async-start | bytes 4325376 | tf_op jit(solution)/shard_map/all_gather | solution.py:121
  8.6 250.5 %all-gather.7.cloned.1.call-start = ((), (), s32[]{:S(2)}) async-start(), calls=%async_computation.4 | async-start | bytes 2162688 | tf_op jit(solution)/shard_map/all_gather | solution.py:122
  15.6 23.6 %all-to-all-start = ((bf16[32,2,2048]{2,1,0:T(2,128)(2,1)}), bf16[32,2,2048]{2,1,0:T(2,128)(2,1)S(1)}, u32[]{:S(2)}, u32[]{:S(2)}) async-start(bf16[32,2,2048]{2,1,0:T(2,128)(2,1)} %reshape.889), calls=%async_computation | async-start | bytes 524288 | tf_op jit(solution)/shard_map/all_to_all | solution.py:136
  39.2 16.9 %all-to-all-start.1 = ((bf16[32,2,2048]{2,1,0:T(2,128)(2,1)}), bf16[32,2,2048]{2,1,0:T(2,128)(2,1)S(1)}, u32[]{:S(2)}, u32[]{:S(2)}) async-start(bf16[32,2,2048]{2,1,0:T(2,128)(2,1)} %reshape.891), calls=%async_computation.1 | async-start | bytes 524288 | tf_op jit(solution)/shard_map/all_to_all | solution.py:136
  56.1 18.4 %all-to-all-start.2 = ((bf16[32,2,2048]{2,1,0:T(2,128)(2,1)}), bf16[32,2,2048]{2,1,0:T(2,128)(2,1)S(1)}, u32[]{:S(2)}, u32[]{:S(2)}) async-start(bf16[32,2,2048]{2,1,0:T(2,128)(2,1)} %reshape.893), calls=%async_computation.2 | async-start | bytes 524288 | tf_op jit(solution)/shard_map/all_to_all | solution.py:136
  74.5 18.3 %all-to-all-start.3 = ((bf16[32,2,2048]{2,1,0:T(2,128)(2,1)}), bf16[32,2,2048]{2,1,0:T(2,128)(2,1)S(1)}, u32[]{:S(2)}, u32[]{:S(2)}) async-start(bf16[32,2,2048]{2,1,0:T(2,128)(2,1)} %reshape.895), calls=%async_computation.3 | async-start | bytes 524288 | tf_op jit(solution)/shard_map/all_to_all | solution.py:136
  327.0 17.6 %collective-permute-start = (bf16[32,2048]{1,0:T(8,128)(2,1)S(1)}, bf16[32,2048]{1,0:T(8,128)(2,1)S(1)}, u32[]{:S(2)}, u32[]{:S(2)}) collective-permute-start(bf16[32,2048]{1,0:T(8,128)(2,1)S(1)} %get-tuple-element.1094), channel_id=1, source_target_pairs={{0,32},{32,64},{64,96},{96,128},{128,160},{160,192},{192,224},{1,3... | collective-permute-start | bytes 393224 | tf_op jit(solution)/shard_map/while/body/eval_jaxpr/ppermute | solution.py:15
  345.9 6.3 collective-permute-start
  353.6 17.6 %collective-permute-start = (bf16[32,2048]{1,0:T(8,128)(2,1)S(1)}, bf16[32,2048]{1,0:T(8,128)(2,1)S(1)}, u32[]{:S(2)}, u32[]{:S(2)}) collective-permute-start(bf16[32,2048]{1,0:T(8,128)(2,1)S(1)} %get-tuple-element.1094), channel_id=1, source_target_pairs={{0,32},{32,64},{64,96},{96,128},{128,160},{160,192},{192,224},{1,3... | collective-permute-start | bytes 393224 | tf_op jit(solution)/shard_map/while/body/eval_jaxpr/ppermute | solution.py:15
  372.5 6.3 collective-permute-start
  380.2 11.1 %collective-permute-start = (bf16[32,2048]{1,0:T(8,128)(2,1)S(1)}, bf16[32,2048]{1,0:T(8,128)(2,1)S(1)}, u32[]{:S(2)}, u32[]{:S(2)}) collective-permute-start(bf16[32,2048]{1,0:T(8,128)(2,1)S(1)} %get-tuple-element.1094), channel_id=1, source_target_pairs={{0,32},{32,64},{64,96},{96,128},{128,160},{160,192},{192,224},{1,3... | collective-permute-start | bytes 393224 | tf_op jit(solution)/shard_map/while/body/eval_jaxpr/ppermute | solution.py:15
  392.7 6.3 collective-permute-start
  400.4 15.1 %collective-permute-start = (bf16[32,2048]{1,0:T(8,128)(2,1)S(1)}, bf16[32,2048]{1,0:T(8,128)(2,1)S(1)}, u32[]{:S(2)}, u32[]{:S(2)}) collective-permute-start(bf16[32,2048]{1,0:T(8,128)(2,1)S(1)} %get-tuple-element.1094), channel_id=1, source_target_pairs={{0,32},{32,64},{64,96},{96,128},{128,160},{160,192},{192,224},{1,3... | collective-permute-start | bytes 393224 | tf_op jit(solution)/shard_map/while/body/eval_jaxpr/ppermute | solution.py:15
  418.8 6.3 collective-permute-start.1
  427.7 12.0 %collective-permute-start.1 = (bf16[32,2048]{1,0:T(8,128)(2,1)}, bf16[32,2048]{1,0:T(8,128)(2,1)S(1)}, u32[]{:S(2)}, u32[]{:S(2)}) collective-permute-start(bf16[32,2048]{1,0:T(8,128)(2,1)} %get-tuple-element.977), channel_id=1, source_target_pairs={{32,0},{64,32},{96,64},{128,96},{160,128},{192,160},{224,192},{33,... | collective-permute-start | bytes 393224 | tf_op jit(solution)/shard_map/while/body/eval_jaxpr/ppermute | solution.py:15
  442.2 6.5 collective-permute-start.1
  451.2 15.9 %collective-permute-start.1 = (bf16[32,2048]{1,0:T(8,128)(2,1)}, bf16[32,2048]{1,0:T(8,128)(2,1)S(1)}, u32[]{:S(2)}, u32[]{:S(2)}) collective-permute-start(bf16[32,2048]{1,0:T(8,128)(2,1)} %get-tuple-element.977), channel_id=1, source_target_pairs={{32,0},{64,32},{96,64},{128,96},{160,128},{192,160},{224,192},{33,... | collective-permute-start | bytes 393224 | tf_op jit(solution)/shard_map/while/body/eval_jaxpr/ppermute | solution.py:15
  469.6 6.5 collective-permute-start.1
  478.5 11.9 %collective-permute-start.1 = (bf16[32,2048]{1,0:T(8,128)(2,1)}, bf16[32,2048]{1,0:T(8,128)(2,1)S(1)}, u32[]{:S(2)}, u32[]{:S(2)}) collective-permute-start(bf16[32,2048]{1,0:T(8,128)(2,1)} %get-tuple-element.977), channel_id=1, source_target_pairs={{32,0},{64,32},{96,64},{128,96},{160,128},{192,160},{224,192},{33,... | collective-permute-start | bytes 393224 | tf_op jit(solution)/shard_map/while/body/eval_jaxpr/ppermute | solution.py:15
  492.9 210.5 %collective-permute-start.1 = (bf16[32,2048]{1,0:T(8,128)(2,1)}, bf16[32,2048]{1,0:T(8,128)(2,1)S(1)}, u32[]{:S(2)}, u32[]{:S(2)}) collective-permute-start(bf16[32,2048]{1,0:T(8,128)(2,1)} %get-tuple-element.977), channel_id=1, source_target_pairs={{32,0},{64,32},{96,64},{128,96},{160,128},{192,160},{224,192},{33,... | collective-permute-start | bytes 393224 | tf_op jit(solution)/shard_map/while/body/eval_jaxpr/ppermute | solution.py:15
  735.6 6.5 collective-permute-start.1
  774.2 6.5 collective-permute-start.1
  812.9 6.5 collective-permute-start.1
  (68 other events, 434.7 us)
Sparse Core Ops, SparseCore 0:
  10.6 89.3 all-gather.10
  102.5 79.0 all-gather.8
  184.2 74.8 all-gather.6
where the time goes:
time: 940 us; the launch traced here: 935 us
  waiting for transfers between devices  471 us (50%)
  starting transfers between devices  124 us (13%)
  matrix products  117 us (12%)
  blocking collectives  73.4 us (8%)
  local copies, waits for them, and re-layouts  68.4 us (7%)
  other arithmetic  50.3 us (5%)
  loops' own time  16.6 us (2%)
  between operations  14 us (1%)
    ppermute x22, waiting for transfers between devices, shifted(): return lax.ppermute(block, axis, route)  274 us
    ppermute x22, starting transfers between devices, shifted(): return lax.ppermute(block, axis, route)  99.3 us
    all_gather x1, waiting for transfers between devices, body(): lax.all_gather(w_query[0], 'dp', axis=0, tiled=True)  75.2 us
    psum x1, blocking collectives, body(): total = lax.psum(grad_sum, 'dp')  73.4 us
    all_gather x1, waiting for transfers between devices, body(): lax.all_gather(w_keyval[0], 'dp', axis=0, tiled=True)  71 us
    all_to_all x4, waiting for transfers between devices, body(): lax.all_to_all(packed, 'dp', split_axis=0, concat_axis=0, tiled=True)  42.1 us
    dot_general x12, matrix products, layer(): jnp.dot(normed, w_query, preferred_element_type=jnp.float32)  42 us
    dot_general x8, matrix products, layer(): jnp.dot(mixed_heads, w_out, preferred_element_type=jnp.float32)  26.5 us
  transfers between devices with their start and end apart: 29, of which 29 were waited for; matrix products, arithmetic and copies ran while one was open for 5% of the time, Pallas kernels for 0%

commit v1 on v0

--- a/solution.py
+++ b/solution.py
@@ -207,7 +207,9 @@
         (zero_block, jnp.zeros_like(steering)),
         jnp.arange(step_count, dtype=jnp.int32),
     )
-    total = lax.psum(grad_sum, "dp")
+    total = grad_sum
+    for hop in (1, 2, 4, 8, 16):
+        total = total + lax.ppermute(total, "dp", [(dev, dev ^ hop) for dev in range(32)])
     return (produced[None], total[None])
 
 

time: 940 us -> 900 us (0.957)
  blocking collectives: 73.4 us -> 0 us
  waiting for transfers between devices: 471 us -> 489 us
    psum x1 -> x0, blocking collectives: 73.4 us -> none  [body(): total = lax.psum(grad_sum, 'dp')]
    ppermute x0 -> x5, waiting for transfers between devices: none -> 18.6 us  [body(): lax.ppermute(total, 'dp', [(dev, dev ^ hop) for dev in range(32)])]
  transfers between devices with their start and end apart: 29 -> 34, of which waited for: 29 -> 34; matrix products, arithmetic and copies ran while one was open for 5% -> 5% of each run, Pallas kernels for 0% -> 0%
where the time goes in v1:
time: 900 us; the launch traced here: 895 us
  waiting for transfers between devices  489 us (54%)
  starting transfers between devices  130 us (14%)
  matrix products  118 us (13%)
  local copies, waits for them, and re-layouts  73.2 us (8%)
  other arithmetic  54.7 us (6%)
  loops' own time  16.7 us (2%)
  between operations  14 us (2%)
    ppermute x22, waiting for transfers between devices, shifted(): return lax.ppermute(block, axis, route)  274 us
    ppermute x22, starting transfers between devices, shifted(): return lax.ppermute(block, axis, route)  99.3 us
    all_gather x1, waiting for transfers between devices, body(): lax.all_gather(w_query[0], 'dp', axis=0, tiled=True)  74.5 us
    all_gather x1, waiting for transfers between devices, body(): lax.all_gather(w_keyval[0], 'dp', axis=0, tiled=True)  71 us
    dot_general x12, matrix products, layer(): jnp.dot(normed, w_query, preferred_element_type=jnp.float32)  42.1 us
    all_to_all x4, waiting for transfers between devices, body(): lax.all_to_all(packed, 'dp', split_axis=0, concat_axis=0, tiled=True)  42 us
    dot_general x8, matrix products, layer(): jnp.dot(mixed_heads, w_out, preferred_element_type=jnp.float32)  26.5 us
    all_to_all x4, starting transfers between devices, body(): lax.all_to_all(packed, 'dp', split_axis=0, concat_axis=0, tiled=True)  24.4 us
  transfers between devices with their start and end apart: 34, of which 34 were waited for; matrix products, arithmetic and copies ran while one was open for 5% of the time, Pallas kernels for 0%

profile of v1, /device:TPU:0, one launch (start us, length us, event | category | flops | bytes accessed | tf_op | source)
XLA Modules:
  0.0 894.9 jit_solution(15918314702832459678)
XLA Ops:
  15.6 9.8 %all-to-all-start = ((bf16[32,2,2048]{2,1,0:T(2,128)(2,1)}), bf16[32,2,2048]{2,1,0:T(2,128)(2,1)S(1)}, u32[]{:S(2)}, u32[]{:S(2)}) async-start(bf16[32,2,2048]{2,1,0:T(2,128)(2,1)} %reshape.889), calls=%async_computation | async-start | bytes 524288 | tf_op jit(solution)/shard_map/all_to_all | solution.py:136
  29.3 9.8 %all-to-all-done = bf16[32,2,2048]{2,1,0:T(2,128)(2,1)S(1)} async-done(((bf16[32,2,2048]{2,1,0:T(2,128)(2,1)}), bf16[32,2,2048]{2,1,0:T(2,128)(2,1)S(1)}, u32[]{:S(2)}, u32[]{:S(2)}) %all-to-all-start) | async-done | bytes 262176 | tf_op jit(solution)/shard_map/all_to_all | solution.py:136
  46.0 10.1 %all-to-all-done.1 = bf16[32,2,2048]{2,1,0:T(2,128)(2,1)S(1)} async-done(((bf16[32,2,2048]{2,1,0:T(2,128)(2,1)}), bf16[32,2,2048]{2,1,0:T(2,128)(2,1)S(1)}, u32[]{:S(2)}, u32[]{:S(2)}) %all-to-all-start.1) | async-done | bytes 262176 | tf_op jit(solution)/shard_map/all_to_all | solution.py:136
  62.5 12.1 %all-to-all-done.2 = bf16[32,2,2048]{2,1,0:T(2,128)(2,1)S(1)} async-done(((bf16[32,2,2048]{2,1,0:T(2,128)(2,1)}), bf16[32,2,2048]{2,1,0:T(2,128)(2,1)S(1)}, u32[]{:S(2)}, u32[]{:S(2)}) %all-to-all-start.2) | async-done | bytes 262176 | tf_op jit(solution)/shard_map/all_to_all | solution.py:136
  82.5 10.0 %all-to-all-done.3 = bf16[32,2,2048]{2,1,0:T(2,128)(2,1)S(1)} async-done(((bf16[32,2,2048]{2,1,0:T(2,128)(2,1)}), bf16[32,2,2048]{2,1,0:T(2,128)(2,1)S(1)}, u32[]{:S(2)}, u32[]{:S(2)}) %all-to-all-start.3) | async-done | bytes 262176 | tf_op jit(solution)/shard_map/all_to_all | solution.py:136
  106.9 74.5 %all-gather.9.cloned.1.call-done = bf16[1,2048,1024]{2,1,0:T(8,128)(2,1)} async-done(((bf16[1,64,1024]{2,1,0:T(8,128)(2,1)}), bf16[1,2048,1024]{2,1,0:T(8,128)(2,1)}) %all-gather.9.cloned.1.call-update) | async-done | bytes 4194320 | tf_op jit(solution)/shard_map/all_gather | solution.py:121
  187.9 71.0 %all-gather.7.cloned.1.call-done = bf16[1,2048,512]{2,1,0:T(8,128)(2,1)} async-done(((bf16[1,64,512]{2,1,0:T(8,128)(2,1)}), bf16[1,2048,512]{2,1,0:T(8,128)(2,1)}) %all-gather.7.cloned.1.call-update) | async-done | bytes 2097168 | tf_op jit(solution)/shard_map/all_gather | solution.py:122
  259.1 156.2 %while.30 = (s32[]{:T(128)}, bf16[32,2048]{1,0:T(8,128)(2,1)S(1)}, bf16[4,32,2048]{2,1,0:T(8,128)(2,1)S(1)}, bf16[4,32,2048]{2,1,0:T(8,128)(2,1)S(1)}, s32[11]{0...) while((s32[]{:T(128)}, bf16[32,2048]{1,0:T(8,128)(2,1)S(1)}, ...), condition=%wide.region_14.15_spmd, body=%wide.region_8.14_spmd.sunk | while | flops 343888544 | bytes 14992390 | solution.py:174
  260.4 11.3 %conditional.5 = (bf16[32,2048]{1,0:T(8,128)(2,1)S(1)}) conditional(s32[]{:T(128)} %convert_element_type.419, () %tuple.130, (bf16[32,2048]{1,0:T(8,128)(2,1)S(1)}, f32[1,2048]{1,0:T(1,128)S(1)}, f32[1,2048]{1,0:T(1,128)S(1)}, bf16[2048,512]{1,0:T(8,128)(2,1)}, s32[4,32]{1,0:T(4,128)}, /*index=5*/s32[]{:T(128)}, s32[4,32]{1,0:T(4,128)}, ...), branch_computations={%region_9.9_spmd, %region_10.13_spmd} | conditional | flops 343691936 | bytes 12894860 | solution.py:159
  275.3 11.3 %conditional.5 = (bf16[32,2048]{1,0:T(8,128)(2,1)S(1)}) conditional(s32[]{:T(128)} %convert_element_type.419, () %tuple.130, (bf16[32,2048]{1,0:T(8,128)(2,1)S(1)}, f32[1,2048]{1,0:T(1,128)S(1)}, f32[1,2048]{1,0:T(1,128)S(1)}, bf16[2048,512]{1,0:T(8,128)(2,1)}, s32[4,32]{1,0:T(4,128)}, /*index=5*/s32[]{:T(128)}, s32[4,32]{1,0:T(4,128)}, ...), branch_computations={%region_9.9_spmd, %region_10.13_spmd} | conditional | flops 343691936 | bytes 12894860 | solution.py:159
  291.2 11.3 %conditional.5 = (bf16[32,2048]{1,0:T(8,128)(2,1)S(1)}) conditional(s32[]{:T(128)} %convert_element_type.419, () %tuple.130, (bf16[32,2048]{1,0:T(8,128)(2,1)S(1)}, f32[1,2048]{1,0:T(1,128)S(1)}, f32[1,2048]{1,0:T(1,128)S(1)}, bf16[2048,512]{1,0:T(8,128)(2,1)}, s32[4,32]{1,0:T(4,128)}, /*index=5*/s32[]{:T(128)}, s32[4,32]{1,0:T(4,128)}, ...), branch_computations={%region_9.9_spmd, %region_10.13_spmd} | conditional | flops 343691936 | bytes 12894860 | solution.py:159
  307.7 11.3 %conditional.5 = (bf16[32,2048]{1,0:T(8,128)(2,1)S(1)}) conditional(s32[]{:T(128)} %convert_element_type.419, () %tuple.130, (bf16[32,2048]{1,0:T(8,128)(2,1)S(1)}, f32[1,2048]{1,0:T(1,128)S(1)}, f32[1,2048]{1,0:T(1,128)S(1)}, bf16[2048,512]{1,0:T(8,128)(2,1)}, s32[4,32]{1,0:T(4,128)}, /*index=5*/s32[]{:T(128)}, s32[4,32]{1,0:T(4,128)}, ...), branch_computations={%region_9.9_spmd, %region_10.13_spmd} | conditional | flops 343691936 | bytes 12894860 | solution.py:159
  326.7 16.6 %collective-permute-start = (bf16[32,2048]{1,0:T(8,128)(2,1)S(1)}, bf16[32,2048]{1,0:T(8,128)(2,1)S(1)}, u32[]{:S(2)}, u32[]{:S(2)}) collective-permute-start(bf16[32,2048]{1,0:T(8,128)(2,1)S(1)} %get-tuple-element.1094), channel_id=1, source_target_pairs={{0,32},{32,64},{64,96},{96,128},{128,160},{160,192},{192,224},{1,3... | collective-permute-start | bytes 393224 | tf_op jit(solution)/shard_map/while/body/eval_jaxpr/ppermute | solution.py:15
  353.3 16.6 %collective-permute-start = (bf16[32,2048]{1,0:T(8,128)(2,1)S(1)}, bf16[32,2048]{1,0:T(8,128)(2,1)S(1)}, u32[]{:S(2)}, u32[]{:S(2)}) collective-permute-start(bf16[32,2048]{1,0:T(8,128)(2,1)S(1)} %get-tuple-element.1094), channel_id=1, source_target_pairs={{0,32},{32,64},{64,96},{96,128},{128,160},{160,192},{192,224},{1,3... | collective-permute-start | bytes 393224 | tf_op jit(solution)/shard_map/while/body/eval_jaxpr/ppermute | solution.py:15
  379.9 10.2 %collective-permute-start = (bf16[32,2048]{1,0:T(8,128)(2,1)S(1)}, bf16[32,2048]{1,0:T(8,128)(2,1)S(1)}, u32[]{:S(2)}, u32[]{:S(2)}) collective-permute-start(bf16[32,2048]{1,0:T(8,128)(2,1)S(1)} %get-tuple-element.1094), channel_id=1, source_target_pairs={{0,32},{32,64},{64,96},{96,128},{128,160},{160,192},{192,224},{1,3... | collective-permute-start | bytes 393224 | tf_op jit(solution)/shard_map/while/body/eval_jaxpr/ppermute | solution.py:15
  400.1 14.2 %collective-permute-start = (bf16[32,2048]{1,0:T(8,128)(2,1)S(1)}, bf16[32,2048]{1,0:T(8,128)(2,1)S(1)}, u32[]{:S(2)}, u32[]{:S(2)}) collective-permute-start(bf16[32,2048]{1,0:T(8,128)(2,1)S(1)} %get-tuple-element.1094), channel_id=1, source_target_pairs={{0,32},{32,64},{64,96},{96,128},{128,160},{160,192},{192,224},{1,3... | collective-permute-start | bytes 393224 | tf_op jit(solution)/shard_map/while/body/eval_jaxpr/ppermute | solution.py:15
  416.0 446.1 %while.31 = (s32[]{:T(128)}, bf16[32,2048]{1,0:T(8,128)(2,1)S(1)}, f32[2048]{0:T(1024)}, s32[11]{0:T(128)}, s32[]{:T(128)}, /*index=5*/pred[]{:T(512)}, bf16[4,3...) while((s32[]{:T(128)}, bf16[32,2048]{1,0:T(8,128)(2,1)S(1)}, ...), condition=%wide.region_26.27_spmd.clone, body=%wide.region_15.26_spmd.clone.sunk | while | flops 551212288 | bytes 31677904 | solution.py:205
  431.3 9.4 %collective-permute-done.1 = bf16[32,2048]{1,0:T(8,128)(2,1)S(1)} collective-permute-done((bf16[32,2048]{1,0:T(8,128)(2,1)}, bf16[32,2048]{1,0:T(8,128)(2,1)S(1)}, u32[]{:S(2)}, u32[]{:S(2)}) %collective-permute-start.1) | collective-permute-done | bytes 131104 | tf_op jit(solution)/shard_map/while/body/eval_jaxpr/ppermute | solution.py:15
  456.1 13.3 %collective-permute-done.1 = bf16[32,2048]{1,0:T(8,128)(2,1)S(1)} collective-permute-done((bf16[32,2048]{1,0:T(8,128)(2,1)}, bf16[32,2048]{1,0:T(8,128)(2,1)S(1)}, u32[]{:S(2)}, u32[]{:S(2)}) %collective-permute-start.1) | collective-permute-done | bytes 131104 | tf_op jit(solution)/shard_map/while/body/eval_jaxpr/ppermute | solution.py:15
  499.7 208.1 %collective-permute-done.1 = bf16[32,2048]{1,0:T(8,128)(2,1)S(1)} collective-permute-done((bf16[32,2048]{1,0:T(8,128)(2,1)}, bf16[32,2048]{1,0:T(8,128)(2,1)S(1)}, u32[]{:S(2)}, u32[]{:S(2)}) %collective-permute-start.1) | collective-permute-done | bytes 131104 | tf_op jit(solution)/shard_map/while/body/eval_jaxpr/ppermute | solution.py:15
  709.7 31.0 %conditional.6 = (bf16[32,2048]{1,0:T(8,128)(2,1)}, f32[2048]{0:T(1024)}) conditional(s32[]{:T(128)} %convert_element_type.420, () %tuple.133, (pred[]{:T(512)}, s32[]{:T(128)}, bf16[4,32,2048]{2,1,0:T(8,128)(2,1)}, bf16[32,2048]{1,0:T(8,128)(2,1)S(1)}, bf16[1024,2048]{1,0:T(8,128)(2,1)}, /*index=5*/s32[4,32]{1,0:T(4,128)}, ...), branch_computations={%region_16.16_spmd, %region_17.25_spmd} | conditional | flops 551208192 | bytes 31128680 | solution.py:199
  749.1 31.0 %conditional.6 = (bf16[32,2048]{1,0:T(8,128)(2,1)}, f32[2048]{0:T(1024)}) conditional(s32[]{:T(128)} %convert_element_type.420, () %tuple.133, (pred[]{:T(512)}, s32[]{:T(128)}, bf16[4,32,2048]{2,1,0:T(8,128)(2,1)}, bf16[32,2048]{1,0:T(8,128)(2,1)S(1)}, bf16[1024,2048]{1,0:T(8,128)(2,1)}, /*index=5*/s32[4,32]{1,0:T(4,128)}, ...), branch_computations={%region_16.16_spmd, %region_17.25_spmd} | conditional | flops 551208192 | bytes 31128680 | solution.py:199
  788.4 31.0 %conditional.6 = (bf16[32,2048]{1,0:T(8,128)(2,1)}, f32[2048]{0:T(1024)}) conditional(s32[]{:T(128)} %convert_element_type.420, () %tuple.133, (pred[]{:T(512)}, s32[]{:T(128)}, bf16[4,32,2048]{2,1,0:T(8,128)(2,1)}, bf16[32,2048]{1,0:T(8,128)(2,1)S(1)}, bf16[1024,2048]{1,0:T(8,128)(2,1)}, /*index=5*/s32[4,32]{1,0:T(4,128)}, ...), branch_computations={%region_16.16_spmd, %region_17.25_spmd} | conditional | flops 551208192 | bytes 31128680 | solution.py:199
  827.7 31.0 %conditional.6 = (bf16[32,2048]{1,0:T(8,128)(2,1)}, f32[2048]{0:T(1024)}) conditional(s32[]{:T(128)} %convert_element_type.420, () %tuple.133, (pred[]{:T(512)}, s32[]{:T(128)}, bf16[4,32,2048]{2,1,0:T(8,128)(2,1)}, bf16[32,2048]{1,0:T(8,128)(2,1)S(1)}, bf16[1024,2048]{1,0:T(8,128)(2,1)}, /*index=5*/s32[4,32]{1,0:T(4,128)}, ...), branch_computations={%region_16.16_spmd, %region_17.25_spmd} | conditional | flops 551208192 | bytes 31128680 | solution.py:199
  (611 shorter events, 387.7 us)
Async XLA Ops:
  7.2 93.2 %all-gather.11.cloned.1.call-start = ((), (), s32[]{:S(2)}) async-start(), calls=%async_computation.6 | async-start | bytes 4325376 | tf_op jit(solution)/shard_map/all_gather | solution.py:123
  7.9 173.5 %all-gather.9.cloned.1.call-start = ((), (), s32[]{:S(2)}) async-start(), calls=%async_computation.5 | async-start | bytes 4325376 | tf_op jit(solution)/shard_map/all_gather | solution.py:121
  8.6 250.3 %all-gather.7.cloned.1.call-start = ((), (), s32[]{:S(2)}) async-start(), calls=%async_computation.4 | async-start | bytes 2162688 | tf_op jit(solution)/shard_map/all_gather | solution.py:122
  15.6 23.6 %all-to-all-start = ((bf16[32,2,2048]{2,1,0:T(2,128)(2,1)}), bf16[32,2,2048]{2,1,0:T(2,128)(2,1)S(1)}, u32[]{:S(2)}, u32[]{:S(2)}) async-start(bf16[32,2,2048]{2,1,0:T(2,128)(2,1)} %reshape.889), calls=%async_computation | async-start | bytes 524288 | tf_op jit(solution)/shard_map/all_to_all | solution.py:136
  39.2 17.0 %all-to-all-start.1 = ((bf16[32,2,2048]{2,1,0:T(2,128)(2,1)}), bf16[32,2,2048]{2,1,0:T(2,128)(2,1)S(1)}, u32[]{:S(2)}, u32[]{:S(2)}) async-start(bf16[32,2,2048]{2,1,0:T(2,128)(2,1)} %reshape.891), calls=%async_computation.1 | async-start | bytes 524288 | tf_op jit(solution)/shard_map/all_to_all | solution.py:136
  56.1 18.5 %all-to-all-start.2 = ((bf16[32,2,2048]{2,1,0:T(2,128)(2,1)}), bf16[32,2,2048]{2,1,0:T(2,128)(2,1)S(1)}, u32[]{:S(2)}, u32[]{:S(2)}) async-start(bf16[32,2,2048]{2,1,0:T(2,128)(2,1)} %reshape.893), calls=%async_computation.2 | async-start | bytes 524288 | tf_op jit(solution)/shard_map/all_to_all | solution.py:136
  74.6 17.9 %all-to-all-start.3 = ((bf16[32,2,2048]{2,1,0:T(2,128)(2,1)}), bf16[32,2,2048]{2,1,0:T(2,128)(2,1)S(1)}, u32[]{:S(2)}, u32[]{:S(2)}) async-start(bf16[32,2,2048]{2,1,0:T(2,128)(2,1)} %reshape.895), calls=%async_computation.3 | async-start | bytes 524288 | tf_op jit(solution)/shard_map/all_to_all | solution.py:136
  319.1 6.3 collective-permute-start
  326.7 17.6 %collective-permute-start = (bf16[32,2048]{1,0:T(8,128)(2,1)S(1)}, bf16[32,2048]{1,0:T(8,128)(2,1)S(1)}, u32[]{:S(2)}, u32[]{:S(2)}) collective-permute-start(bf16[32,2048]{1,0:T(8,128)(2,1)S(1)} %get-tuple-element.1094), channel_id=1, source_target_pairs={{0,32},{32,64},{64,96},{96,128},{128,160},{160,192},{192,224},{1,3... | collective-permute-start | bytes 393224 | tf_op jit(solution)/shard_map/while/body/eval_jaxpr/ppermute | solution.py:15
  353.3 17.6 %collective-permute-start = (bf16[32,2048]{1,0:T(8,128)(2,1)S(1)}, bf16[32,2048]{1,0:T(8,128)(2,1)S(1)}, u32[]{:S(2)}, u32[]{:S(2)}) collective-permute-start(bf16[32,2048]{1,0:T(8,128)(2,1)S(1)} %get-tuple-element.1094), channel_id=1, source_target_pairs={{0,32},{32,64},{64,96},{96,128},{128,160},{160,192},{192,224},{1,3... | collective-permute-start | bytes 393224 | tf_op jit(solution)/shard_map/while/body/eval_jaxpr/ppermute | solution.py:15
  372.3 6.3 collective-permute-start
  379.9 11.1 %collective-permute-start = (bf16[32,2048]{1,0:T(8,128)(2,1)S(1)}, bf16[32,2048]{1,0:T(8,128)(2,1)S(1)}, u32[]{:S(2)}, u32[]{:S(2)}) collective-permute-start(bf16[32,2048]{1,0:T(8,128)(2,1)S(1)} %get-tuple-element.1094), channel_id=1, source_target_pairs={{0,32},{32,64},{64,96},{96,128},{128,160},{160,192},{192,224},{1,3... | collective-permute-start | bytes 393224 | tf_op jit(solution)/shard_map/while/body/eval_jaxpr/ppermute | solution.py:15
  400.1 15.1 %collective-permute-start = (bf16[32,2048]{1,0:T(8,128)(2,1)S(1)}, bf16[32,2048]{1,0:T(8,128)(2,1)S(1)}, u32[]{:S(2)}, u32[]{:S(2)}) collective-permute-start(bf16[32,2048]{1,0:T(8,128)(2,1)S(1)} %get-tuple-element.1094), channel_id=1, source_target_pairs={{0,32},{32,64},{64,96},{96,128},{128,160},{160,192},{192,224},{1,3... | collective-permute-start | bytes 393224 | tf_op jit(solution)/shard_map/while/body/eval_jaxpr/ppermute | solution.py:15
  419.2 6.3 collective-permute-start.1
  428.7 12.0 %collective-permute-start.1 = (bf16[32,2048]{1,0:T(8,128)(2,1)}, bf16[32,2048]{1,0:T(8,128)(2,1)S(1)}, u32[]{:S(2)}, u32[]{:S(2)}) collective-permute-start(bf16[32,2048]{1,0:T(8,128)(2,1)} %get-tuple-element.977), channel_id=1, source_target_pairs={{32,0},{64,32},{96,64},{128,96},{160,128},{192,160},{224,192},{33,... | collective-permute-start | bytes 393224 | tf_op jit(solution)/shard_map/while/body/eval_jaxpr/ppermute | solution.py:15
  443.9 6.5 collective-permute-start.1
  453.5 15.9 %collective-permute-start.1 = (bf16[32,2048]{1,0:T(8,128)(2,1)}, bf16[32,2048]{1,0:T(8,128)(2,1)S(1)}, u32[]{:S(2)}, u32[]{:S(2)}) collective-permute-start(bf16[32,2048]{1,0:T(8,128)(2,1)} %get-tuple-element.977), channel_id=1, source_target_pairs={{32,0},{64,32},{96,64},{128,96},{160,128},{192,160},{224,192},{33,... | collective-permute-start | bytes 393224 | tf_op jit(solution)/shard_map/while/body/eval_jaxpr/ppermute | solution.py:15
  472.5 6.5 collective-permute-start.1
  482.1 11.9 %collective-permute-start.1 = (bf16[32,2048]{1,0:T(8,128)(2,1)}, bf16[32,2048]{1,0:T(8,128)(2,1)S(1)}, u32[]{:S(2)}, u32[]{:S(2)}) collective-permute-start(bf16[32,2048]{1,0:T(8,128)(2,1)} %get-tuple-element.977), channel_id=1, source_target_pairs={{32,0},{64,32},{96,64},{128,96},{160,128},{192,160},{224,192},{33,... | collective-permute-start | bytes 393224 | tf_op jit(solution)/shard_map/while/body/eval_jaxpr/ppermute | solution.py:15
  497.1 210.8 %collective-permute-start.1 = (bf16[32,2048]{1,0:T(8,128)(2,1)}, bf16[32,2048]{1,0:T(8,128)(2,1)S(1)}, u32[]{:S(2)}, u32[]{:S(2)}) collective-permute-start(bf16[32,2048]{1,0:T(8,128)(2,1)} %get-tuple-element.977), channel_id=1, source_target_pairs={{32,0},{64,32},{96,64},{128,96},{160,128},{192,160},{224,192},{33,... | collective-permute-start | bytes 393224 | tf_op jit(solution)/shard_map/while/body/eval_jaxpr/ppermute | solution.py:15
  740.7 6.5 collective-permute-start.1
  780.1 6.5 collective-permute-start.1
  819.4 6.5 collective-permute-start.1
  871.4 7.6 collective-permute-start.4
  (73 other events, 458.5 us)
Sparse Core Ops, SparseCore 0:
  10.6 89.7 all-gather.10
  103.0 78.3 all-gather.8
  184.0 74.8 all-gather.6
